TPU v7x, 256 devices: a whole 4x4x8 slice. The times are simulated.
256 devices in a mesh: tm: 4 (over y), row: 4 (over x), col: 16 (over z, core).
Axes of the slice: x: 4, y: 4, z: 8, core: 2. Of those that a mesh axis runs over, the one named last changes fastest.
Arguments:
- day_block: float32 [4, 4, 16, 32, 4, 4, 128], P('tm', None, 'col', None, None, 'row'), as said below
- left_coupling: float32 [4, 4, 16, 32, 4, 4, 128], P('tm', None, 'col', None, None, 'row'), may hold values from -0.125 to 0.125
- right_coupling: float32 [4, 4, 16, 32, 4, 4, 128], P('tm', None, 'col', None, None, 'row'), may hold values from -0.125 to 0.125
- separator_block: float32 [4, 4, 16, 32, 4, 4, 128], P('tm', None, 'col', None, None, 'row')
- arrow_coupling: float32 [4, 4, 16, 32, 64], P('tm', None, 'col'), may hold values from -0.125 to 0.125
- arrow_block: float32 [64, 64], replicated
Outputs:
- day_factor: float32 [4, 4, 16, 32, 4, 4, 128], P('tm', None, 'col', None, None, 'row')
- left_factor: float32 [4, 4, 16, 32, 4, 4, 128], P('tm', None, 'col', None, None, 'row')
- right_factor: float32 [4, 4, 16, 32, 4, 4, 128], P('tm', None, 'col', None, None, 'row')
- arrow_factor: float32 [4, 4, 16, 32, 64], P('tm', None, 'col')
- separator: float32 [4, 4, 16, 32, 4, 4, 128], P('tm', None, 'col', None, None, 'row')
- arrowhead: float32 [64, 64], replicated
Inputs may be any that keep to these rules, and one draw needn't show every extreme that they name: Each group's day_block and separator_block, and arrow_block, is an exactly symmetric matrix with all eigenvalues at least 1.
All inputs are finite; a program needn't handle non-finite values.
Results may differ from a plain program's by a relative error of at most 0.0001.
Values sent between devices are 32-bit elements; how exact they have to be, the bound alone decides.
No kernel may reach another device: no remote copies, remote signals or barrier semaphores. Data moves between devices by JAX's collectives and lax.ppermute only.
A program may use at most 128 MiB of HBM per device.

v0:
```python
import jax
import jax.numpy as jnp
from jax import lax
from jax.sharding import PartitionSpec as P


def passed_along(value, axis, steps):
    count = lax.axis_size(axis)
    initial, last = (max(0, -steps), min(count, count - steps))
    return lax.ppermute(value, axis, [(source, source + steps) for source in range(initial, last)])


def product(left, right):
    return jnp.dot(left, right, precision=lax.Precision.HIGHEST, preferred_element_type=jnp.float32)


def lower_inverse(factor):
    identity = jnp.eye(factor.shape[0], dtype=jnp.float32)
    return lax.linalg.triangular_solve(factor, identity, left_side=True, lower=True)


def reorder_nodes(whole, panels, col_width):
    count = whole.shape[0]
    col_count = lax.axis_size("col")
    spread = whole.reshape(count, panels, col_count, col_width)
    return jnp.transpose(spread, (2, 1, 3, 0)).reshape(col_count * panels * col_width, count)


def separator_term(solved, panels, col_width, row_width):
    whole = lax.all_gather(
        solved.reshape(solved.shape[0], panels, 1, row_width), "row", axis=2, tiled=True
    )
    ordered = reorder_nodes(whole, panels, col_width)
    return lax.psum_scatter(product(ordered, solved), "col", scatter_dimension=0, tiled=True)


def per_device(
    day_block, left_coupling, right_coupling, separator_block, arrow_coupling, arrow_block
):
    panels = day_block.shape[1]
    col_width = day_block.shape[3]
    row_width = day_block.shape[6]
    panel_size = col_width * lax.axis_size("col")
    arrow_rows = arrow_block.shape[0]
    col_index = lax.axis_index("col")
    row_index = lax.axis_index("row")
    matrix = day_block.reshape(panels, col_width, panels, row_width)
    left_part = left_coupling.reshape(panels, col_width, panels, row_width)
    right_part = right_coupling.reshape(panels, col_width, panels, row_width)
    arrow_part = arrow_coupling.reshape(panels, col_width, arrow_rows)
    rows_at = col_index * col_width + lax.broadcasted_iota(jnp.int32, (col_width, row_width), 0)
    cols_at = row_index * row_width + lax.broadcasted_iota(jnp.int32, (col_width, row_width), 1)
    factor_blocks = []
    left_blocks = []
    right_blocks = []
    arrow_blocks = []
    for current in range(panels):
        remain = panels - current
        gathered_day, gathered_left, gathered_right, gathered_arrow = (
            lax.all_gather(matrix[current, :, current:, :], "col", axis=0, tiled=True),
            lax.all_gather(left_part[current], "col", axis=0, tiled=True),
            lax.all_gather(right_part[current], "col", axis=0, tiled=True),
            lax.all_gather(arrow_part[current], "col", axis=0, tiled=True),
        )
        diagonal_full = lax.all_gather(gathered_day[:, 0:1, :], "row", axis=1, tiled=True).reshape(
            panel_size, panel_size
        )
        factor = jnp.linalg.cholesky(diagonal_full)
        inverse = lower_inverse(factor)
        owned = product(inverse, gathered_day.reshape(panel_size, remain * row_width)).reshape(
            panel_size, remain, row_width
        )
        if remain > 1:
            later = lax.all_gather(owned[:, 1:, None, :], "row", axis=2, tiled=True).reshape(
                panel_size, remain - 1, panel_size
            )
        solved_left = product(inverse, gathered_left.reshape(panel_size, panels * row_width))
        solved_right = product(inverse, gathered_right.reshape(panel_size, panels * row_width))
        solved_arrow = product(inverse, gathered_arrow)
        mine_rows = lax.dynamic_slice_in_dim(owned, col_index * col_width, col_width, 0)
        diagonal_part = jnp.where(cols_at >= rows_at, mine_rows[:, 0, :], 0.0)
        factor_blocks.append(
            jnp.concatenate(
                [
                    jnp.zeros((col_width, current, row_width), jnp.float32),
                    diagonal_part[:, None, :],
                    mine_rows[:, 1:, :],
                ],
                axis=1,
            )
        )
        left_blocks.append(
            lax.dynamic_slice_in_dim(solved_left, col_index * col_width, col_width, 0)
        )
        right_blocks.append(
            lax.dynamic_slice_in_dim(solved_right, col_index * col_width, col_width, 0)
        )
        arrow_blocks.append(
            lax.dynamic_slice_in_dim(solved_arrow, col_index * col_width, col_width, 0)
        )
        if remain > 1:
            mine_later = lax.dynamic_slice_in_dim(later, col_index * col_width, col_width, 2)
            mine_later = mine_later.reshape(panel_size, (remain - 1) * col_width).T
            owned_later = owned[:, 1:, :].reshape(panel_size, (remain - 1) * row_width)
            matrix = matrix.at[current + 1 :, :, current + 1 :, :].add(
                -product(mine_later, owned_later).reshape(
                    remain - 1, col_width, remain - 1, row_width
                )
            )
            left_part = left_part.at[current + 1 :].add(
                -product(mine_later, solved_left).reshape(remain - 1, col_width, panels, row_width)
            )
            right_part = right_part.at[current + 1 :].add(
                -product(mine_later, solved_right).reshape(remain - 1, col_width, panels, row_width)
            )
            arrow_part = arrow_part.at[current + 1 :].add(
                -product(mine_later, solved_arrow).reshape(remain - 1, col_width, arrow_rows)
            )
    day_factor = jnp.stack(factor_blocks).reshape(day_block.shape)
    left_solved = jnp.stack(left_blocks).reshape(panels * col_width, panels * row_width)
    right_solved = jnp.stack(right_blocks).reshape(panels * col_width, panels * row_width)
    arrow_solved = jnp.stack(arrow_blocks).reshape(panels * col_width, arrow_rows)
    separator_local = separator_block.reshape(panels * col_width, panels * row_width)
    right_term = separator_term(right_solved, panels, col_width, row_width)
    left_term = separator_term(left_solved, panels, col_width, row_width)
    from_next = passed_along(left_term, "tm", -1)
    separator = separator_local - right_term - from_next
    arrow_local = product(arrow_solved.T, arrow_solved)
    arrow_total = lax.psum(arrow_local, ("tm", "col"))
    arrowhead = arrow_block - arrow_total
    return (
        day_factor,
        left_solved.reshape(left_coupling.shape),
        right_solved.reshape(right_coupling.shape),
        arrow_solved.reshape(arrow_coupling.shape),
        separator.reshape(separator_block.shape),
        arrowhead,
    )


def solution(mesh):
    return jax.shard_map(
        per_device,
        mesh=mesh,
        in_specs=(
            P("tm", None, "col", None, None, "row", None),
            P("tm", None, "col", None, None, "row", None),
            P("tm", None, "col", None, None, "row", None),
            P("tm", None, "col", None, None, "row", None),
            P("tm", None, "col", None, None),
            P(),
        ),
        out_specs=(
            P("tm", None, "col", None, None, "row", None),
            P("tm", None, "col", None, None, "row", None),
            P("tm", None, "col", None, None, "row", None),
            P("tm", None, "col", None, None),
            P("tm", None, "col", None, None, "row", None),
            P(),
        ),
        check_vma=False,
    )
```

profile of v0, /device:TPU:4, one launch (start us, length us, event | category | flops | bytes accessed | tf_op | source)
XLA Modules:
  0.0 1516.8 jit_solution(10383593552836481364)
XLA Ops:
  8.8 43.1 %all-gather.49.cloned.1.call-done = f32[1,1,1,512,4,1,128]{6,4,5,2,1,0,3:T(4,128)} async-done(((f32[1,1,1,32,4,1,128]{6,4,5,2,1,0,3:T(4,128)}), f32[1,1,1,512,4,1,128]{6,4,5,2,1,0,3:T(4,128)}) %all-gather.49.cloned.1.call-update) | async-done | bytes 1048592 | tf_op jit(solution)/shard_map/all_gather | solution.py:60
  56.8 21.8 %all-gather.39.cloned.1.call-done = f32[512,4,128]{2,0,1:T(8,128)} async-done(((f32[512,1,128]{2,0,1:T(8,128)}), f32[512,4,128]{2,0,1:T(8,128)}) %all-gather.39.cloned.1.call-update) | async-done | bytes 1048592 | tf_op jit(solution)/shard_map/all_gather | solution.py:65
  81.7 11.7 cholesky.462
  93.4 9.8 custom-call.35
  105.9 11.7 cholesky.481
  117.7 10.2 custom-call.36
  129.5 11.7 cholesky.502
  141.9 9.8 custom-call.37
  153.1 11.9 cholesky.519
  169.1 8.0 while.20
  177.1 39.3 %custom-call.38 = f32[4,128,128]{1,2,0:T(8,128)S(1)} custom-call(f32[4,128,128]{2,1,0:T(8,128)S(1)} %get-tuple-element.178), custom_call_target="InvertDiagBlocksLowerTriangular" | custom-call | tf_op jit(solution)/shard_map/triangular_solve/custom-call.3 | solution.py:19
  228.2 44.8 %all-gather.51.cloned.1.call-done = f32[512,3,512]{2,0,1:T(8,128)} async-done(((f32[512,3,128]{2,0,1:T(8,128)}), f32[512,3,512]{2,0,1:T(8,128)}) %all-gather.51.cloned.1.call-update) | async-done | bytes 3145744 | tf_op jit(solution)/shard_map/all_gather | solution.py:74
  278.2 19.6 %all-gather.2 = f32[1,512,3,128]{3,1,2,0:T(8,128)S(1)} all-gather(f32[1,32,3,128]{3,1,2,0:T(8,128)S(1)} %slice.678), channel_id=4, replica_groups=mesh['tm'=4,'row'=4,'col'=16] {'col'}, dimensions={1}, use_global_device_ids=true | all-gather | bytes 835584 | tf_op jit(solution)/shard_map/all_gather | solution.py:60
  299.9 23.1 %all-gather.41.cloned.1.call-done = f32[512,4,128]{2,0,1:T(8,128)} async-done(((f32[512,1,128]{2,0,1:T(8,128)}), f32[512,4,128]{2,0,1:T(8,128)}) %all-gather.41.cloned.1.call-update) | async-done | bytes 1048592 | tf_op jit(solution)/shard_map/all_gather | solution.py:65
  328.3 11.7 cholesky.534
  340.7 9.8 custom-call.39
  353.1 11.7 cholesky.553
  365.5 10.2 custom-call.40
  377.3 11.7 cholesky.574
  389.7 9.8 custom-call.41
  401.0 11.9 cholesky.591
  417.3 11.6 while.21
  428.9 39.3 %custom-call.42 = f32[4,128,128]{1,2,0:T(8,128)S(1)} custom-call(f32[4,128,128]{2,1,0:T(8,128)S(1)} %get-tuple-element.179), custom_call_target="InvertDiagBlocksLowerTriangular" | custom-call | tf_op jit(solution)/shard_map/triangular_solve/custom-call.3 | solution.py:19
  485.7 32.4 %all-gather.53.cloned.1.call-done = f32[512,2,512]{2,0,1:T(8,128)} async-done(((f32[512,2,128]{2,0,1:T(8,128)}), f32[512,2,512]{2,0,1:T(8,128)}) %all-gather.53.cloned.1.call-update) | async-done | bytes 2097168 | tf_op jit(solution)/shard_map/all_gather | solution.py:74
  523.1 19.0 %all-gather.4 = f32[1,512,2,128]{3,1,2,0:T(8,128)S(1)} all-gather(f32[1,32,2,128]{3,1,2,0:T(8,128)S(1)} %slice.689), channel_id=6, replica_groups=mesh['tm'=4,'row'=4,'col'=16] {'col'}, dimensions={1}, use_global_device_ids=true | all-gather | bytes 557056 | tf_op jit(solution)/shard_map/all_gather | solution.py:60
  543.7 16.5 %all-gather.59.cloned.1.call-done = f32[1,1,1,512,4,1,128]{6,4,5,2,1,0,3:T(4,128)} async-done(((f32[1,1,1,32,4,1,128]{6,4,5,2,1,0,3:T(4,128)}), f32[1,1,1,512,4,1,128]{6,4,5,2,1,0,3:T(4,128)}) %all-gather.59.cloned.1.call-update) | async-done | bytes 1048592 | tf_op jit(solution)/shard_map/all_gather | solution.py:61
  571.5 27.8 %all-gather.67.cloned.1.call-done = f32[1,1,1,512,4,1,128]{6,4,5,2,1,0,3:T(4,128)} async-done(((f32[1,1,1,32,4,1,128]{6,4,5,2,1,0,3:T(4,128)}), f32[1,1,1,512,4,1,128]{6,4,5,2,1,0,3:T(4,128)}) %all-gather.67.cloned.1.call-update) | async-done | bytes 1048592 | tf_op jit(solution)/shard_map/all_gather | solution.py:62
  610.8 15.2 %all-gather.43.cloned.1.call-done = f32[512,4,128]{2,0,1:T(8,128)} async-done(((f32[512,1,128]{2,0,1:T(8,128)}), f32[512,4,128]{2,0,1:T(8,128)}) %all-gather.43.cloned.1.call-update) | async-done | bytes 1048592 | tf_op jit(solution)/shard_map/all_gather | solution.py:65
  631.1 11.7 cholesky.606
  643.5 9.8 custom-call.43
  656.7 11.7 cholesky.625
  669.1 10.0 custom-call.44
  681.5 11.7 cholesky.646
  693.9 9.8 custom-call.45
  705.2 11.9 cholesky.663
  721.4 11.5 while.22
  732.9 39.3 %custom-call.46 = f32[4,128,128]{1,2,0:T(8,128)S(1)} custom-call(f32[4,128,128]{2,1,0:T(8,128)S(1)} %get-tuple-element.180), custom_call_target="InvertDiagBlocksLowerTriangular" | custom-call | tf_op jit(solution)/shard_map/triangular_solve/custom-call.3 | solution.py:19
  786.9 4.1 fusion.196
  800.3 4.0 fusion.195
  815.3 19.6 %all-gather.6 = f32[1,512,1,128]{3,1,2,0:T(8,128)} all-gather(f32[1,32,1,128]{3,1,2,0:T(8,128)S(1)} %fusion.15), channel_id=8, replica_groups=mesh['tm'=4,'row'=4,'col'=16] {'col'}, dimensions={1}, use_global_device_ids=true | all-gather | bytes 278528 | tf_op jit(solution)/shard_map/all_gather | solution.py:60
  835.0 18.0 %all-gather.63.cloned.1.call-done = f32[1,512,4,128]{3,1,2,0:T(8,128)} async-done(((f32[1,32,4,128]{3,1,2,0:T(8,128)}), f32[1,512,4,128]{3,1,2,0:T(8,128)}) %all-gather.63.cloned.1.call-update) | async-done | bytes 1048592 | tf_op jit(solution)/shard_map/all_gather | solution.py:61
  855.6 4.1 fusion.194
  868.1 24.0 %all-gather.71.cloned.1.call-done = f32[1,512,4,128]{3,1,2,0:T(8,128)} async-done(((f32[1,32,4,128]{3,1,2,0:T(8,128)}), f32[1,512,4,128]{3,1,2,0:T(8,128)}) %all-gather.71.cloned.1.call-update) | async-done | bytes 1048592 | tf_op jit(solution)/shard_map/all_gather | solution.py:62
  894.7 4.1 fusion.193
  904.6 13.5 all-gather.57.cloned.1.call-done
  923.3 11.7 cholesky.678
  935.7 10.4 custom-call.47
  951.0 13.2 cholesky.697
  966.3 11.5 custom-call.48
  981.5 13.2 cholesky.718
  996.9 11.3 custom-call.49
  1011.1 13.6 cholesky.735
  1029.8 11.6 while.23
  1041.4 39.3 %custom-call.50 = f32[4,128,128]{1,2,0:T(8,128)S(1)} custom-call(f32[4,128,128]{2,1,0:T(8,128)S(1)} %get-tuple-element.181), custom_call_target="InvertDiagBlocksLowerTriangular" | custom-call | tf_op jit(solution)/shard_map/triangular_solve/custom-call.3 | solution.py:19
  1105.5 16.4 %all-gather.47.cloned.1.call-done = f32[128,4,4,128]{3,0,1,2:T(8,128)} async-done(((f32[128,4,1,128]{3,0,1,2:T(8,128)}), f32[128,4,4,128]{3,0,1,2:T(8,128)}) %all-gather.47.cloned.1.call-update) | async-done | bytes 1048592 | tf_op jit(solution)/shard_map/all_gather | solution.py:30
  1123.6 5.0 fusion.202
  1128.8 21.8 %all-gather.45.cloned.1.call-done = f32[128,4,4,128]{3,0,1,2:T(8,128)} async-done(((f32[128,4,1,128]{3,0,1,2:T(8,128)}), f32[128,4,4,128]{3,0,1,2:T(8,128)}) %all-gather.45.cloned.1.call-update) | async-done | bytes 1048592 | tf_op jit(solution)/shard_map/all_gather | solution.py:30
  1152.4 5.0 fusion.201
  1157.9 18.1 %all-gather.16 = f32[1,1,1,512,64]{4,3,2,1,0:T(8,128)S(1)} all-gather(f32[1,1,1,32,64]{4,3,2,1,0:T(8,128)S(1)} %slice-done.1), channel_id=18, replica_groups=mesh['tm'=4,'row'=4,'col'=16] {'col'}, dimensions={3}, use_global_device_ids=true | all-gather | bytes 139264 | tf_op jit(solution)/shard_map/all_gather | solution.py:63
  1185.0 16.1 %all-gather.17 = f32[1,512,64]{2,1,0:T(8,128)S(1)} all-gather(f32[1,32,64]{2,1,0:T(8,128)S(1)} %slice.716), channel_id=19, replica_groups=mesh['tm'=4,'row'=4,'col'=16] {'col'}, dimensions={1}, use_global_device_ids=true | all-gather | bytes 139264 | tf_op jit(solution)/shard_map/all_gather | solution.py:63
  1206.7 16.0 %all-gather.18 = f32[1,512,64]{2,1,0:T(8,128)S(1)} all-gather(f32[1,32,64]{2,1,0:T(8,128)S(1)} %slice.718), channel_id=20, replica_groups=mesh['tm'=4,'row'=4,'col'=16] {'col'}, dimensions={1}, use_global_device_ids=true | all-gather | bytes 139264 | tf_op jit(solution)/shard_map/all_gather | solution.py:63
  1228.6 15.9 %all-gather.19 = f32[1,512,64]{2,1,0:T(8,128)S(1)} all-gather(f32[1,32,64]{2,1,0:T(8,128)S(1)} %fusion.13), channel_id=21, replica_groups=mesh['tm'=4,'row'=4,'col'=16] {'col'}, dimensions={1}, use_global_device_ids=true | all-gather | bytes 139264 | tf_op jit(solution)/shard_map/all_gather | solution.py:63
  1247.9 249.4 %psum.7 = f32[64,64]{1,0:T(8,128)S(1)} all-reduce(f32[64,64]{1,0:T(8,128)S(1)} %convolution_bitcast_fusion), channel_id=1, replica_groups=mesh['tm'=4,'row'=4,'col'=16] {'tm','col'}, use_global_device_ids=true, to_apply=%region_10.0 | all-reduce | flops 4096 | bytes 32768 | tf_op jit(solution)/shard_map/psum | solution.py:129
  1503.7 4.3 collective-permute-done
  (478 shorter events, 294.7 us)
Async XLA Ops:
  7.2 44.7 %all-gather.49.cloned.1.call-start = ((), (), s32[]{:S(2)}) async-start(), calls=%async_computation.9 | async-start | bytes 1114112 | tf_op jit(solution)/shard_map/all_gather | solution.py:60
  8.7 69.9 %all-gather.39.cloned.1.call-start = ((), (), s32[]{:S(2)}) async-start(), calls=%async_computation.2 | async-start | bytes 1310720 | tf_op jit(solution)/shard_map/all_gather | solution.py:65
  54.0 218.9 %all-gather.51.cloned.1.call-start = ((), (), s32[]{:S(2)}) async-start(), calls=%async_computation.10 | async-start | bytes 3932160 | tf_op jit(solution)/shard_map/all_gather | solution.py:74
  177.1 39.8 %copy-start.23 = (f32[512,512]{1,0:T(8,128)}, f32[512,512]{1,0:T(8,128)S(1)}, u32[]{:S(2)}) copy-start(f32[512,512]{1,0:T(8,128)S(1)} %get-tuple-element.505) | copy-start | bytes 3145732
  219.0 7.7 copy-start.59
  219.4 379.8 %copy-start = (f32[128,512]{1,0:T(8,128)}, f32[128,512]{1,0:T(8,128)S(1)}, u32[]{:S(2)}) copy-start(f32[128,512]{1,0:T(8,128)S(1)} %fusion.151) | copy-start | bytes 786436
  221.5 53.7 %copy-start.11 = (f32[128,512]{1,0:T(8,128)}, f32[128,512]{1,0:T(8,128)S(1)}, u32[]{:S(2)}) copy-start(f32[128,512]{1,0:T(8,128)S(1)} %fusion.150) | copy-start | bytes 786436
  226.7 96.3 %all-gather.41.cloned.1.call-start = ((), (), s32[]{:S(2)}) async-start(), calls=%async_computation.3 | async-start | bytes 1310720 | tf_op jit(solution)/shard_map/all_gather | solution.py:65
  276.6 328.2 %copy-start.9 = (f32[512,3,32]{0,2,1:T(8,128)}, f32[512,3,32]{0,2,1:T(8,128)S(1)}, u32[]{:S(2)}) copy-start(f32[512,3,32]{0,2,1:T(8,128)S(1)} %copy.124) | copy-start | bytes 589828
  298.5 219.6 %all-gather.53.cloned.1.call-start = ((), (), s32[]{:S(2)}) async-start(), calls=%async_computation.11 | async-start | bytes 2621440 | tf_op jit(solution)/shard_map/all_gather | solution.py:74
  468.2 3.4 copy-start.50
  472.1 48.0 %copy-start.2 = (f32[128,512]{1,0:T(8,128)}, f32[128,512]{1,0:T(8,128)S(1)}, u32[]{:S(2)}) copy-start(f32[128,512]{1,0:T(8,128)S(1)} %fusion.145) | copy-start | bytes 786436
  479.6 80.6 %copy-start.12 = (f32[128,512]{1,0:T(8,128)S(1)}, f32[128,512]{1,0:T(8,128)}, u32[]{:S(2)}) copy-start(f32[128,512]{1,0:T(8,128)} %copy-done.11) | copy-start | bytes 786436
  480.5 79.7 %all-gather.59.cloned.1.call-start = ((), (), s32[]{:S(2)}) async-start(), calls=%async_computation.14 | async-start | bytes 1114112 | tf_op jit(solution)/shard_map/all_gather | solution.py:61
  482.0 117.2 %all-gather.67.cloned.1.call-start = ((), (), s32[]{:S(2)}) async-start(), calls=%async_computation.18 | async-start | bytes 1114112 | tf_op jit(solution)/shard_map/all_gather | solution.py:62
  483.6 142.4 %all-gather.43.cloned.1.call-start = ((), (), s32[]{:S(2)}) async-start(), calls=%async_computation.4 | async-start | bytes 1310720 | tf_op jit(solution)/shard_map/all_gather | solution.py:65
  520.1 46.6 %slice-start = ((f32[1,4,1,32,4,1,128]{6,5,4,3,2,1,0:T(1,128)}), f32[1,3,1,32,4,1,128]{6,5,4,3,2,1,0:T(1,128)S(1)}, s32[]{:S(2)}) async-start(f32[1,4,1,32,4,1,128]{6,5,4,3,2,1,0:T(1,128)} %param.34), calls=%async_computation.22 | async-start | bytes 393216 | tf_op jit(solution)/shard_map/slice.420
  523.0 46.1 %copy-start.57 = (f32[2,32,2,128]{3,1,2,0:T(8,128)}, f32[2,32,2,128]{3,1,2,0:T(8,128)S(1)}, u32[]{:S(2)}) copy-start(f32[2,32,2,128]{3,1,2,0:T(8,128)S(1)} %fusion.9) | copy-start | bytes 196612
  543.6 240.8 %all-gather.61.cloned.1.call-start = ((), (), s32[]{:S(2)}) async-start(), calls=%async_computation.15 | async-start | bytes 1114112 | tf_op jit(solution)/shard_map/all_gather | solution.py:61
  569.1 34.2 %copy-start.39 = (f32[3,32,4,128]{3,1,2,0:T(8,128)}, f32[3,32,4,128]{3,1,2,0:T(8,128)S(1)}, u32[]{:S(2)}) copy-start(f32[3,32,4,128]{3,1,2,0:T(8,128)S(1)} %fusion) | copy-start | bytes 589828
  569.8 227.9 %all-gather.69.cloned.1.call-start = ((), (), s32[]{:S(2)}) async-start(), calls=%async_computation.19 | async-start | bytes 1114112 | tf_op jit(solution)/shard_map/all_gather | solution.py:62
  608.3 203.2 %all-gather.55.cloned.1.call-start = ((), (), s32[]{:S(2)}) async-start(), calls=%async_computation.12 | async-start | bytes 1310720 | tf_op jit(solution)/shard_map/all_gather | solution.py:74
  774.3 120.3 %copy-start.5 = (f32[128,512]{1,0:T(8,128)}, f32[128,512]{1,0:T(8,128)S(1)}, u32[]{:S(2)}) copy-start(f32[128,512]{1,0:T(8,128)S(1)} %fusion.141) | copy-start | bytes 786436
  774.3 12.6 copy-start.3
  774.4 12.6 copy-start.15
  777.1 117.6 %copy-start.17 = (f32[128,512]{1,0:T(8,128)}, f32[128,512]{1,0:T(8,128)S(1)}, u32[]{:S(2)}) copy-start(f32[128,512]{1,0:T(8,128)S(1)} %fusion.139) | copy-start | bytes 786436
  784.3 68.7 %all-gather.63.cloned.1.call-start = ((), (), s32[]{:S(2)}) async-start(), calls=%async_computation.16 | async-start | bytes 1114112 | tf_op jit(solution)/shard_map/all_gather | solution.py:61
  797.2 94.9 %all-gather.71.cloned.1.call-start = ((), (), s32[]{:S(2)}) async-start(), calls=%async_computation.20 | async-start | bytes 1114112 | tf_op jit(solution)/shard_map/all_gather | solution.py:62
  804.3 51.2 %copy-start.29 = (f32[128,512]{1,0:T(8,128)S(1)}, f32[128,512]{1,0:T(8,128)}, u32[]{:S(2)}) copy-start(f32[128,512]{1,0:T(8,128)} %copy-done.28) | copy-start | bytes 786436
  809.3 50.4 %copy-start.45 = (f32[2,32,4,128]{3,1,2,0:T(8,128)}, f32[2,32,4,128]{3,1,2,0:T(8,128)S(1)}, u32[]{:S(2)}) copy-start(f32[2,32,4,128]{3,1,2,0:T(8,128)S(1)} %fusion.3) | copy-start | bytes 393220
  810.0 108.1 %all-gather.57.cloned.1.call-start = ((), (), s32[]{:S(2)}) async-start(), calls=%async_computation.13 | async-start | bytes 1310720 | tf_op jit(solution)/shard_map/all_gather | solution.py:65
  814.0 48.1 %copy-start.47 = (f32[2,32,4,128]{3,1,2,0:T(8,128)S(1)}, f32[2,32,4,128]{3,1,2,0:T(8,128)}, u32[]{:S(2)}) copy-start(f32[2,32,4,128]{3,1,2,0:T(8,128)} %copy-done.46) | copy-start | bytes 393220
  834.9 253.6 %all-gather.65.cloned.1.call-start = ((), (), s32[]{:S(2)}) async-start(), calls=%async_computation.17 | async-start | bytes 1114112 | tf_op jit(solution)/shard_map/all_gather | solution.py:61
  865.1 234.1 %all-gather.73.cloned.1.call-start = ((), (), s32[]{:S(2)}) async-start(), calls=%async_computation.21 | async-start | bytes 1114112 | tf_op jit(solution)/shard_map/all_gather | solution.py:62
  904.3 217.6 %all-gather.47.cloned.1.call-start = ((), (), s32[]{:S(2)}) async-start(), calls=%async_computation.7 | async-start | bytes 1310720 | tf_op jit(solution)/shard_map/all_gather | solution.py:30
  1082.8 18.0 %copy-start.7 = (f32[128,512]{1,0:T(8,128)}, f32[128,512]{1,0:T(8,128)S(1)}, u32[]{:S(2)}) copy-start(f32[128,512]{1,0:T(8,128)S(1)} %fusion.135) | copy-start | bytes 786436
  1085.5 15.3 %copy-start.19 = (f32[128,512]{1,0:T(8,128)}, f32[128,512]{1,0:T(8,128)S(1)}, u32[]{:S(2)}) copy-start(f32[128,512]{1,0:T(8,128)S(1)} %fusion.133) | copy-start | bytes 786436
  1088.5 12.4 copy-start.31
  1093.9 5.3 copy-start.33
  1094.8 55.9 %all-gather.45.cloned.1.call-start = ((), (), s32[]{:S(2)}) async-start(), calls=%async_computation.5 | async-start | bytes 1310720 | tf_op jit(solution)/shard_map/all_gather | solution.py:30
  1103.7 19.9 %copy-start.34 = (f32[4,32,512]{2,1,0:T(8,128)S(1)}, f32[4,32,512]{2,1,0:T(8,128)}, u32[]{:S(2)}) copy-start(f32[4,32,512]{2,1,0:T(8,128)} %copy-done.33) | copy-start | bytes 786436
  1105.5 394.0 %reduce-scatter.5.cloned.1.call-start = ((), (), s32[]{:S(2)}) async-start(), calls=%async_computation.8 | async-start | bytes 4456448 | tf_op jit(solution)/shard_map/reduce_scatter | solution.py:34
  1128.6 375.0 %reduce-scatter.3.cloned.1.call-start = ((), (), s32[]{:S(2)}) async-start(), calls=%async_computation.6 | async-start | bytes 4456448 | tf_op jit(solution)/shard_map/reduce_scatter | solution.py:34
  1152.3 5.6 slice-start.1
  1152.3 24.8 %copy-start.1 = (f32[128,512]{1,0:T(8,128)S(1)}, f32[128,512]{1,0:T(8,128)}, u32[]{:S(2)}) copy-start(f32[128,512]{1,0:T(8,128)} %copy-done) | copy-start | bytes 786436
  1152.3 24.8 %copy-start.13 = (f32[128,512]{1,0:T(8,128)S(1)}, f32[128,512]{1,0:T(8,128)}, u32[]{:S(2)}) copy-start(f32[128,512]{1,0:T(8,128)} %copy-done.11) | copy-start | bytes 786436
  1157.4 25.8 %copy-start.10 = (f32[512,3,32]{0,2,1:T(8,128)S(1)}, f32[512,3,32]{0,2,1:T(8,128)}, u32[]{:S(2)}) copy-start(f32[512,3,32]{0,2,1:T(8,128)} %copy-done.9) | copy-start | bytes 589828
  1157.4 43.7 %copy-start.4 = (f32[128,512]{1,0:T(8,128)S(1)}, f32[128,512]{1,0:T(8,128)}, u32[]{:S(2)}) copy-start(f32[128,512]{1,0:T(8,128)} %copy-done.2) | copy-start | bytes 786436
  1157.4 43.7 %copy-start.16 = (f32[128,512]{1,0:T(8,128)S(1)}, f32[128,512]{1,0:T(8,128)}, u32[]{:S(2)}) copy-start(f32[128,512]{1,0:T(8,128)} %copy-done.14) | copy-start | bytes 786436
  1157.4 65.3 %copy-start.6 = (f32[128,512]{1,0:T(8,128)S(1)}, f32[128,512]{1,0:T(8,128)}, u32[]{:S(2)}) copy-start(f32[128,512]{1,0:T(8,128)} %copy-done.5) | copy-start | bytes 786436
  1157.4 65.3 %copy-start.18 = (f32[128,512]{1,0:T(8,128)S(1)}, f32[128,512]{1,0:T(8,128)}, u32[]{:S(2)}) copy-start(f32[128,512]{1,0:T(8,128)} %copy-done.17) | copy-start | bytes 786436
  1179.0 43.7 %copy-start.30 = (f32[128,512]{1,0:T(8,128)S(1)}, f32[128,512]{1,0:T(8,128)}, u32[]{:S(2)}) copy-start(f32[128,512]{1,0:T(8,128)} %copy-done.28) | copy-start | bytes 786436
  1179.0 65.6 %copy-start.8 = (f32[128,512]{1,0:T(8,128)S(1)}, f32[128,512]{1,0:T(8,128)}, u32[]{:S(2)}) copy-start(f32[128,512]{1,0:T(8,128)} %copy-done.7) | copy-start | bytes 786436
  1179.0 65.6 %copy-start.20 = (f32[128,512]{1,0:T(8,128)S(1)}, f32[128,512]{1,0:T(8,128)}, u32[]{:S(2)}) copy-start(f32[128,512]{1,0:T(8,128)} %copy-done.19) | copy-start | bytes 786436
  1179.0 65.6 %copy-start.32 = (f32[128,512]{1,0:T(8,128)S(1)}, f32[128,512]{1,0:T(8,128)}, u32[]{:S(2)}) copy-start(f32[128,512]{1,0:T(8,128)} %copy-done.31) | copy-start | bytes 786436
  1202.2 42.3 %copy-start.38 = (f32[1,512,1,128]{3,1,2,0:T(8,128)S(1)}, f32[1,512,1,128]{3,1,2,0:T(8,128)}, u32[]{:S(2)}) copy-start(f32[1,512,1,128]{3,1,2,0:T(8,128)} %all-gather.6) | copy-start | bytes 786436
  1202.2 43.3 %copy-start.62 = (s32[32]{0:T(128)S(1)}, s32[32]{0:T(128)}, u32[]{:S(2)}) copy-start(s32[32]{0:T(128)} %iota_add_fusion) | copy-start | bytes 388
  1202.3 43.3 %copy-start.63 = (s32[128]{0:T(128)S(1)}, s32[128]{0:T(128)}, u32[]{:S(2)}) copy-start(s32[128]{0:T(128)} %iota_add_fusion.1) | copy-start | bytes 1540
  1222.7 24.9 %copy-start.60 = (f32[32,64]{1,0:T(8,128)S(1)}, f32[32,64]{1,0:T(8,128)}, u32[]{:S(2)}) copy-start(f32[32,64]{1,0:T(8,128)} %copy.156) | copy-start | bytes 24580
  1222.7 274.7 %copy-start.61 = (f32[64,64]{1,0:T(8,128)S(1)}, f32[64,64]{1,0:T(8,128)}, u32[]{:S(2)}) copy-start(f32[64,64]{1,0:T(8,128)} %param.38) | copy-start | bytes 49156
  1223.9 277.9 %copy-start.55 = (f32[1,1,1,32,4,1,128]{6,5,4,3,2,1,0:T(1,128)S(1)}, f32[1,1,1,32,4,1,128]{6,5,4,3,2,1,0:T(1,128)}, u32[]{:S(2)}) copy-start(f32[1,1,1,32,4,1,128]{6,5,4,3,2,1,0:T(1,128)} %stack.85) | copy-start | bytes 196612
  1223.9 278.9 %copy-start.54 = (f32[1,1,1,32,4,1,128]{6,5,4,3,2,1,0:T(1,128)S(1)}, f32[1,1,1,32,4,1,128]{6,5,4,3,2,1,0:T(1,128)}, u32[]{:S(2)}) copy-start(f32[1,1,1,32,4,1,128]{6,5,4,3,2,1,0:T(1,128)} %stack.90) | copy-start | bytes 196612
  1224.9 283.0 %copy-start.53 = (f32[1,4,1,32,4,1,128]{6,5,4,3,2,1,0:T(1,128)S(1)}, f32[1,4,1,32,4,1,128]{6,5,4,3,2,1,0:T(1,128)}, u32[]{:S(2)}) copy-start(f32[1,4,1,32,4,1,128]{6,5,4,3,2,1,0:T(1,128)} %param.36) | copy-start | bytes 786436
  1499.5 8.5 collective-permute-start
  (23 other events, 20.0 us)
Sparse Core Ops, SparseCore 0:
  10.4 41.4 all-gather.48
  54.3 24.2 all-gather.38
  226.8 46.1 all-gather.50
  298.6 24.3 all-gather.40
  480.6 37.4 all-gather.52
  520.3 39.7 all-gather.58
  562.0 37.2 all-gather.66
  601.6 24.2 all-gather.42
  627.8 40.1 all-gather.60
  669.7 37.3 all-gather.68
  784.4 27.0 all-gather.54
  813.2 39.7 all-gather.62
  854.9 37.1 all-gather.70
  893.8 24.2 all-gather.56
  919.8 40.2 all-gather.64
  961.8 37.0 all-gather.72
  1094.9 26.9 all-gather.46
  1123.6 27.0 all-gather.44
  1153.2 65.4 reduce-scatter.4
  1221.1 62.4 reduce-scatter.2
where the time goes:
time: 1530 us; the launch traced here: 1520 us
  other arithmetic  503 us (33%)
  blocking collectives  374 us (24%)
  waiting for transfers between devices  325 us (21%)
  local copies, waits for them, and re-layouts  159 us (10%)
  matrix products  126 us (8%)
  between operations  26.5 us (2%)
    another operation x59, other arithmetic, per_device(): factor = jnp.linalg.cholesky(diagonal_full)  329 us
    psum x1, blocking collectives, per_device(): arrow_total = lax.psum(arrow_local, ('tm', 'col'))  249 us
    another operation x9, other arithmetic, lower_inverse(): lax.linalg.triangular_solve(factor, identity, left_side=True, lower=True)  161 us
    all_gather x3, waiting for transfers between devices, per_device(): lax.all_gather(owned[:, 1:, None, :], 'row', axis=2, tiled=True)  78.6 us
    all_gather x4, waiting for transfers between devices, per_device(): lax.all_gather(gathered_day[:, 0:1, :], 'row', axis=1, tiled=True)  73.6 us
    dot_general x31, matrix products, product(): jnp.dot(left, right, precision=lax.Precision.HIGHEST, preferred_element_t...  73.6 us
    all_gather x4, blocking collectives, per_device(): lax.all_gather(arrow_part[current], 'col', axis=0, tiled=True)  66.2 us
    all_gather x3, blocking collectives, per_device(): lax.all_gather(matrix[current, :, current:, :], 'col', axis=0, tiled=True)  58.2 us
  transfers between devices with their start and end apart: 21, of which 15 were waited for; matrix products, arithmetic and copies ran while one was open for 31% of the time, Pallas kernels for 0%

commit v1 on v0

--- a/solution.py
+++ b/solution.py
@@ -2,6 +2,12 @@
 import jax.numpy as jnp
 from jax import lax
 from jax.sharding import PartitionSpec as P
+
+
+def summed_here(x, axis):
+    shards = lax.all_gather(x, axis, axis=0, tiled=False)
+    total = shards.sum(axis=0)
+    return total
 
 
 def passed_along(value, axis, steps):
@@ -126,7 +132,7 @@
     from_next = passed_along(left_term, "tm", -1)
     separator = separator_local - right_term - from_next
     arrow_local = product(arrow_solved.T, arrow_solved)
-    arrow_total = lax.psum(arrow_local, ("tm", "col"))
+    arrow_total = summed_here(arrow_local, ("tm", "col"))
     arrowhead = arrow_block - arrow_total
     return (
         day_factor,

time: 1530 us -> 1380 us (0.902)
  blocking collectives: 374 us -> 124 us
  waiting for transfers between devices: 325 us -> 431 us
    psum x1 -> x0, blocking collectives: 249 us -> none  [per_device(): arrow_total = lax.psum(arrow_local, ('tm', 'col'))]
    all_gather x0 -> x1, waiting for transfers between devices: none -> 71.3 us  [summed_here(): shards = lax.all_gather(x, axis, axis=0, tiled=False)]
    reduce_scatter x2, waiting for transfers between devices: 0.01 us -> 61 us  [separator_term(): lax.psum_scatter(product(ordered, solved), 'col', scatter_dimension=0, ti...]
    all_gather x2, waiting for transfers between devices: 38.2 us -> 17 us  [separator_term(): lax.all_gather(solved.reshape(solved.shape[0], panels, 1, row_width), 'ro...]
  transfers between devices with their start and end apart: 21 -> 22, of which waited for: 15 -> 15; matrix products, arithmetic and copies ran while one was open for 31% -> 34% of each run, Pallas kernels for 0% -> 0%
where the time goes in v1:
time: 1380 us; the launch traced here: 1370 us
  other arithmetic  501 us (36%)
  waiting for transfers between devices  431 us (31%)
  local copies, waits for them, and re-layouts  157 us (11%)
  matrix products  125 us (9%)
  blocking collectives  124 us (9%)
  between operations  26.6 us (2%)
    another operation x59, other arithmetic, per_device(): factor = jnp.linalg.cholesky(diagonal_full)  329 us
    another operation x9, other arithmetic, lower_inverse(): lax.linalg.triangular_solve(factor, identity, left_side=True, lower=True)  161 us
    all_gather x3, waiting for transfers between devices, per_device(): lax.all_gather(owned[:, 1:, None, :], 'row', axis=2, tiled=True)  78.8 us
    dot_general x31, matrix products, product(): jnp.dot(left, right, precision=lax.Precision.HIGHEST, preferred_element_t...  73.8 us
    all_gather x4, waiting for transfers between devices, per_device(): lax.all_gather(gathered_day[:, 0:1, :], 'row', axis=1, tiled=True)  73.5 us
    all_gather x1, waiting for transfers between devices, summed_here(): shards = lax.all_gather(x, axis, axis=0, tiled=False)  71.3 us
    all_gather x4, blocking collectives, per_device(): lax.all_gather(arrow_part[current], 'col', axis=0, tiled=True)  65.8 us
    reduce_scatter x2, waiting for transfers between devices, separator_term(): lax.psum_scatter(product(ordered, solved), 'col', scatter_dimension=0, ti...  61 us
  transfers between devices with their start and end apart: 22, of which 15 were waited for; matrix products, arithmetic and copies ran while one was open for 34% of the time, Pallas kernels for 0%

profile of v1, /device:TPU:4, one launch (start us, length us, event | category | flops | bytes accessed | tf_op | source)
XLA Modules:
  0.0 1369.1 jit_solution(8451575155954148226)
XLA Ops:
  8.8 43.1 %all-gather.51.cloned.1.call-done = f32[1,1,1,512,4,1,128]{6,4,5,2,1,0,3:T(4,128)} async-done(((f32[1,1,1,32,4,1,128]{6,4,5,2,1,0,3:T(4,128)}), f32[1,1,1,512,4,1,128]{6,4,5,2,1,0,3:T(4,128)}) %all-gather.51.cloned.1.call-update) | async-done | bytes 1048592 | tf_op jit(solution)/shard_map/all_gather | solution.py:66
  56.8 21.8 %all-gather.41.cloned.1.call-done = f32[512,4,128]{2,0,1:T(8,128)} async-done(((f32[512,1,128]{2,0,1:T(8,128)}), f32[512,4,128]{2,0,1:T(8,128)}) %all-gather.41.cloned.1.call-update) | async-done | bytes 1048592 | tf_op jit(solution)/shard_map/all_gather | solution.py:71
  81.7 11.7 cholesky.462
  93.5 9.8 custom-call.35
  105.9 11.7 cholesky.481
  117.7 10.0 custom-call.36
  129.2 11.7 cholesky.502
  141.6 9.8 custom-call.37
  152.8 11.9 cholesky.519
  168.8 8.0 while.20
  176.8 39.3 %custom-call.38 = f32[4,128,128]{1,2,0:T(8,128)S(1)} custom-call(f32[4,128,128]{2,1,0:T(8,128)S(1)} %get-tuple-element.178), custom_call_target="InvertDiagBlocksLowerTriangular" | custom-call | tf_op jit(solution)/shard_map/triangular_solve/custom-call.3 | solution.py:25
  228.0 44.8 %all-gather.53.cloned.1.call-done = f32[512,3,512]{2,0,1:T(8,128)} async-done(((f32[512,3,128]{2,0,1:T(8,128)}), f32[512,3,512]{2,0,1:T(8,128)}) %all-gather.53.cloned.1.call-update) | async-done | bytes 3145744 | tf_op jit(solution)/shard_map/all_gather | solution.py:80
  277.9 19.6 %all-gather.2 = f32[1,512,3,128]{3,1,2,0:T(8,128)S(1)} all-gather(f32[1,32,3,128]{3,1,2,0:T(8,128)S(1)} %slice.678), channel_id=4, replica_groups=mesh['tm'=4,'row'=4,'col'=16] {'col'}, dimensions={1}, use_global_device_ids=true | all-gather | bytes 835584 | tf_op jit(solution)/shard_map/all_gather | solution.py:66
  299.9 22.9 %all-gather.43.cloned.1.call-done = f32[512,4,128]{2,0,1:T(8,128)} async-done(((f32[512,1,128]{2,0,1:T(8,128)}), f32[512,4,128]{2,0,1:T(8,128)}) %all-gather.43.cloned.1.call-update) | async-done | bytes 1048592 | tf_op jit(solution)/shard_map/all_gather | solution.py:71
  328.0 11.7 cholesky.534
  340.4 9.8 custom-call.39
  352.9 11.7 cholesky.553
  365.3 10.0 custom-call.40
  376.8 11.7 cholesky.574
  389.2 9.8 custom-call.41
  400.5 12.1 cholesky.591
  416.9 11.6 while.21
  428.4 39.3 %custom-call.42 = f32[4,128,128]{1,2,0:T(8,128)S(1)} custom-call(f32[4,128,128]{2,1,0:T(8,128)S(1)} %get-tuple-element.179), custom_call_target="InvertDiagBlocksLowerTriangular" | custom-call | tf_op jit(solution)/shard_map/triangular_solve/custom-call.3 | solution.py:25
  484.6 32.4 %all-gather.55.cloned.1.call-done = f32[512,2,512]{2,0,1:T(8,128)} async-done(((f32[512,2,128]{2,0,1:T(8,128)}), f32[512,2,512]{2,0,1:T(8,128)}) %all-gather.55.cloned.1.call-update) | async-done | bytes 2097168 | tf_op jit(solution)/shard_map/all_gather | solution.py:80
  521.9 19.0 %all-gather.4 = f32[1,512,2,128]{3,1,2,0:T(8,128)S(1)} all-gather(f32[1,32,2,128]{3,1,2,0:T(8,128)S(1)} %slice.689), channel_id=6, replica_groups=mesh['tm'=4,'row'=4,'col'=16] {'col'}, dimensions={1}, use_global_device_ids=true | all-gather | bytes 557056 | tf_op jit(solution)/shard_map/all_gather | solution.py:66
  542.5 16.6 %all-gather.61.cloned.1.call-done = f32[1,1,1,512,4,1,128]{6,4,5,2,1,0,3:T(4,128)} async-done(((f32[1,1,1,32,4,1,128]{6,4,5,2,1,0,3:T(4,128)}), f32[1,1,1,512,4,1,128]{6,4,5,2,1,0,3:T(4,128)}) %all-gather.61.cloned.1.call-update) | async-done | bytes 1048592 | tf_op jit(solution)/shard_map/all_gather | solution.py:67
  559.1 4.1 fusion.19
  570.5 27.7 %all-gather.69.cloned.1.call-done = f32[1,1,1,512,4,1,128]{6,4,5,2,1,0,3:T(4,128)} async-done(((f32[1,1,1,32,4,1,128]{6,4,5,2,1,0,3:T(4,128)}), f32[1,1,1,512,4,1,128]{6,4,5,2,1,0,3:T(4,128)}) %all-gather.69.cloned.1.call-update) | async-done | bytes 1048592 | tf_op jit(solution)/shard_map/all_gather | solution.py:68
  609.5 15.4 %all-gather.45.cloned.1.call-done = f32[512,4,128]{2,0,1:T(8,128)} async-done(((f32[512,1,128]{2,0,1:T(8,128)}), f32[512,4,128]{2,0,1:T(8,128)}) %all-gather.45.cloned.1.call-update) | async-done | bytes 1048592 | tf_op jit(solution)/shard_map/all_gather | solution.py:71
  630.1 11.7 cholesky.606
  642.6 9.8 custom-call.43
  655.7 11.7 cholesky.625
  668.1 10.0 custom-call.44
  680.6 11.7 cholesky.646
  693.0 9.8 custom-call.45
  704.3 12.1 cholesky.663
  720.7 12.0 while.22
  732.7 39.3 %custom-call.46 = f32[4,128,128]{1,2,0:T(8,128)S(1)} custom-call(f32[4,128,128]{2,1,0:T(8,128)S(1)} %get-tuple-element.180), custom_call_target="InvertDiagBlocksLowerTriangular" | custom-call | tf_op jit(solution)/shard_map/triangular_solve/custom-call.3 | solution.py:25
  786.0 4.1 fusion.196
  799.1 4.1 fusion.195
  814.3 19.7 %all-gather.6 = f32[1,512,1,128]{3,1,2,0:T(8,128)} all-gather(f32[1,32,1,128]{3,1,2,0:T(8,128)S(1)} %fusion.15), channel_id=8, replica_groups=mesh['tm'=4,'row'=4,'col'=16] {'col'}, dimensions={1}, use_global_device_ids=true | all-gather | bytes 278528 | tf_op jit(solution)/shard_map/all_gather | solution.py:66
  834.1 18.0 %all-gather.65.cloned.1.call-done = f32[1,512,4,128]{3,1,2,0:T(8,128)} async-done(((f32[1,32,4,128]{3,1,2,0:T(8,128)}), f32[1,512,4,128]{3,1,2,0:T(8,128)}) %all-gather.65.cloned.1.call-update) | async-done | bytes 1048592 | tf_op jit(solution)/shard_map/all_gather | solution.py:67
  854.6 4.1 fusion.194
  867.2 24.0 %all-gather.73.cloned.1.call-done = f32[1,512,4,128]{3,1,2,0:T(8,128)} async-done(((f32[1,32,4,128]{3,1,2,0:T(8,128)}), f32[1,512,4,128]{3,1,2,0:T(8,128)}) %all-gather.73.cloned.1.call-update) | async-done | bytes 1048592 | tf_op jit(solution)/shard_map/all_gather | solution.py:68
  893.7 4.1 fusion.193
  903.7 13.5 all-gather.59.cloned.1.call-done
  922.4 11.7 cholesky.678
  934.8 10.4 custom-call.47
  950.0 13.2 cholesky.697
  965.4 11.7 custom-call.48
  980.8 13.2 cholesky.718
  996.2 11.3 custom-call.49
  1010.4 13.3 cholesky.735
  1029.0 11.6 while.23
  1040.5 39.3 %custom-call.50 = f32[4,128,128]{1,2,0:T(8,128)S(1)} custom-call(f32[4,128,128]{2,1,0:T(8,128)S(1)} %get-tuple-element.181), custom_call_target="InvertDiagBlocksLowerTriangular" | custom-call | tf_op jit(solution)/shard_map/triangular_solve/custom-call.3 | solution.py:25
  1103.3 17.0 %all-gather.49.cloned.1.call-done = f32[128,4,4,128]{3,0,1,2:T(8,128)} async-done(((f32[128,4,1,128]{3,0,1,2:T(8,128)}), f32[128,4,4,128]{3,0,1,2:T(8,128)}) %all-gather.49.cloned.1.call-update) | async-done | bytes 1048592 | tf_op jit(solution)/shard_map/all_gather | solution.py:36
  1121.9 5.0 fusion.202
  1127.6 18.1 %all-gather.16 = f32[1,1,1,512,64]{4,3,2,1,0:T(8,128)S(1)} all-gather(f32[1,1,1,32,64]{4,3,2,1,0:T(8,128)S(1)} %slice-done.1), channel_id=18, replica_groups=mesh['tm'=4,'row'=4,'col'=16] {'col'}, dimensions={3}, use_global_device_ids=true | all-gather | bytes 139264 | tf_op jit(solution)/shard_map/all_gather | solution.py:69
  1149.0 15.7 %all-gather.17 = f32[1,512,64]{2,1,0:T(8,128)S(1)} all-gather(f32[1,32,64]{2,1,0:T(8,128)S(1)} %slice.716), channel_id=19, replica_groups=mesh['tm'=4,'row'=4,'col'=16] {'col'}, dimensions={1}, use_global_device_ids=true | all-gather | bytes 139264 | tf_op jit(solution)/shard_map/all_gather | solution.py:69
  1166.3 16.3 %all-gather.18 = f32[1,512,64]{2,1,0:T(8,128)S(1)} all-gather(f32[1,32,64]{2,1,0:T(8,128)S(1)} %slice.718), channel_id=20, replica_groups=mesh['tm'=4,'row'=4,'col'=16] {'col'}, dimensions={1}, use_global_device_ids=true | all-gather | bytes 139264 | tf_op jit(solution)/shard_map/all_gather | solution.py:69
  1185.0 15.7 %all-gather.19 = f32[1,512,64]{2,1,0:T(8,128)S(1)} all-gather(f32[1,32,64]{2,1,0:T(8,128)S(1)} %fusion.13), channel_id=21, replica_groups=mesh['tm'=4,'row'=4,'col'=16] {'col'}, dimensions={1}, use_global_device_ids=true | all-gather | bytes 139264 | tf_op jit(solution)/shard_map/all_gather | solution.py:69
  1204.4 5.0 fusion.201
  1225.4 71.3 %all-gather.77.cloned.1.call-done = f32[4096,64]{1,0:T(8,128)} async-done(((f32[64,64]{1,0:T(8,128)}), f32[4096,64]{1,0:T(8,128)}) %all-gather.77.cloned.1.call-update) | async-done | bytes 1048592 | tf_op jit(solution)/shard_map/all_gather | solution.py:8
  1299.1 61.0 %reduce-scatter.3.cloned.1.call-done = f32[128,512]{1,0:T(8,128)} async-done(((f32[2048,512]{1,0:T(8,128)}), f32[128,512]{1,0:T(8,128)}) %reduce-scatter.3.cloned.1.call-update) | async-done | bytes 262160 | tf_op jit(solution)/shard_map/reduce_scatter | solution.py:40
  (487 shorter events, 286.0 us)
Async XLA Ops:
  7.2 44.7 %all-gather.51.cloned.1.call-start = ((), (), s32[]{:S(2)}) async-start(), calls=%async_computation.9 | async-start | bytes 1114112 | tf_op jit(solution)/shard_map/all_gather | solution.py:66
  8.7 69.9 %all-gather.41.cloned.1.call-start = ((), (), s32[]{:S(2)}) async-start(), calls=%async_computation.2 | async-start | bytes 1310720 | tf_op jit(solution)/shard_map/all_gather | solution.py:71
  54.0 218.7 %all-gather.53.cloned.1.call-start = ((), (), s32[]{:S(2)}) async-start(), calls=%async_computation.10 | async-start | bytes 3932160 | tf_op jit(solution)/shard_map/all_gather | solution.py:80
  176.8 39.8 %copy-start.23 = (f32[512,512]{1,0:T(8,128)}, f32[512,512]{1,0:T(8,128)S(1)}, u32[]{:S(2)}) copy-start(f32[512,512]{1,0:T(8,128)S(1)} %get-tuple-element.506) | copy-start | bytes 3145732
  219.2 379.0 %copy-start = (f32[128,512]{1,0:T(8,128)}, f32[128,512]{1,0:T(8,128)S(1)}, u32[]{:S(2)}) copy-start(f32[128,512]{1,0:T(8,128)S(1)} %fusion.151) | copy-start | bytes 786436
  220.8 5.6 copy-start.65
  221.3 6.7 copy-start.11
  226.4 96.3 %all-gather.43.cloned.1.call-start = ((), (), s32[]{:S(2)}) async-start(), calls=%async_computation.3 | async-start | bytes 1310720 | tf_op jit(solution)/shard_map/all_gather | solution.py:71
  276.4 327.5 %copy-start.9 = (f32[512,3,32]{0,2,1:T(8,128)}, f32[512,3,32]{0,2,1:T(8,128)S(1)}, u32[]{:S(2)}) copy-start(f32[512,3,32]{0,2,1:T(8,128)S(1)} %copy.124) | copy-start | bytes 589828
  298.2 218.7 %all-gather.55.cloned.1.call-start = ((), (), s32[]{:S(2)}) async-start(), calls=%async_computation.11 | async-start | bytes 2621440 | tf_op jit(solution)/shard_map/all_gather | solution.py:80
  467.8 3.4 copy-start.53
  471.6 7.7 copy-start.2
  474.6 3.1 copy-start.14
  479.3 79.8 %copy-start.12 = (f32[128,512]{1,0:T(8,128)S(1)}, f32[128,512]{1,0:T(8,128)}, u32[]{:S(2)}) copy-start(f32[128,512]{1,0:T(8,128)} %copy-done.11) | copy-start | bytes 786436
  479.4 79.7 %all-gather.61.cloned.1.call-start = ((), (), s32[]{:S(2)}) async-start(), calls=%async_computation.14 | async-start | bytes 1114112 | tf_op jit(solution)/shard_map/all_gather | solution.py:67
  480.9 117.3 %all-gather.69.cloned.1.call-start = ((), (), s32[]{:S(2)}) async-start(), calls=%async_computation.18 | async-start | bytes 1114112 | tf_op jit(solution)/shard_map/all_gather | solution.py:68
  482.5 142.4 %all-gather.45.cloned.1.call-start = ((), (), s32[]{:S(2)}) async-start(), calls=%async_computation.4 | async-start | bytes 1310720 | tf_op jit(solution)/shard_map/all_gather | solution.py:71
  521.9 43.9 %copy-start.64 = (f32[2,32,2,128]{3,1,2,0:T(8,128)}, f32[2,32,2,128]{3,1,2,0:T(8,128)S(1)}, u32[]{:S(2)}) copy-start(f32[2,32,2,128]{3,1,2,0:T(8,128)S(1)} %fusion.9) | copy-start | bytes 196612
  541.7 24.1 %slice-start = ((f32[1,4,1,32,4,1,128]{6,5,4,3,2,1,0:T(1,128)}), f32[1,3,1,32,4,1,128]{6,5,4,3,2,1,0:T(1,128)S(1)}, s32[]{:S(2)}) async-start(f32[1,4,1,32,4,1,128]{6,5,4,3,2,1,0:T(1,128)} %param.34), calls=%async_computation.23 | async-start | bytes 393216 | tf_op jit(solution)/shard_map/slice.420
  542.5 241.0 %all-gather.63.cloned.1.call-start = ((), (), s32[]{:S(2)}) async-start(), calls=%async_computation.15 | async-start | bytes 1114112 | tf_op jit(solution)/shard_map/all_gather | solution.py:67
  568.1 34.1 %copy-start.42 = (f32[3,32,4,128]{3,1,2,0:T(8,128)}, f32[3,32,4,128]{3,1,2,0:T(8,128)S(1)}, u32[]{:S(2)}) copy-start(f32[3,32,4,128]{3,1,2,0:T(8,128)S(1)} %fusion) | copy-start | bytes 589828
  568.8 227.7 %all-gather.71.cloned.1.call-start = ((), (), s32[]{:S(2)}) async-start(), calls=%async_computation.19 | async-start | bytes 1114112 | tf_op jit(solution)/shard_map/all_gather | solution.py:68
  607.2 203.3 %all-gather.57.cloned.1.call-start = ((), (), s32[]{:S(2)}) async-start(), calls=%async_computation.12 | async-start | bytes 1310720 | tf_op jit(solution)/shard_map/all_gather | solution.py:80
  772.1 4.0 copy-start.54
  774.1 119.6 %copy-start.5 = (f32[128,512]{1,0:T(8,128)}, f32[128,512]{1,0:T(8,128)S(1)}, u32[]{:S(2)}) copy-start(f32[128,512]{1,0:T(8,128)S(1)} %fusion.141) | copy-start | bytes 786436
  776.0 117.7 %copy-start.17 = (f32[128,512]{1,0:T(8,128)}, f32[128,512]{1,0:T(8,128)S(1)}, u32[]{:S(2)}) copy-start(f32[128,512]{1,0:T(8,128)S(1)} %fusion.139) | copy-start | bytes 786436
  777.7 8.3 copy-start.3
  777.7 8.3 copy-start.15
  783.4 68.7 %all-gather.65.cloned.1.call-start = ((), (), s32[]{:S(2)}) async-start(), calls=%async_computation.16 | async-start | bytes 1114112 | tf_op jit(solution)/shard_map/all_gather | solution.py:67
  796.3 94.9 %all-gather.73.cloned.1.call-start = ((), (), s32[]{:S(2)}) async-start(), calls=%async_computation.20 | async-start | bytes 1114112 | tf_op jit(solution)/shard_map/all_gather | solution.py:68
  805.8 48.9 %copy-start.29 = (f32[128,512]{1,0:T(8,128)S(1)}, f32[128,512]{1,0:T(8,128)}, u32[]{:S(2)}) copy-start(f32[128,512]{1,0:T(8,128)} %copy-done.28) | copy-start | bytes 786436
  808.1 50.6 %copy-start.48 = (f32[2,32,4,128]{3,1,2,0:T(8,128)}, f32[2,32,4,128]{3,1,2,0:T(8,128)S(1)}, u32[]{:S(2)}) copy-start(f32[2,32,4,128]{3,1,2,0:T(8,128)S(1)} %fusion.3) | copy-start | bytes 393220
  808.8 108.3 %all-gather.59.cloned.1.call-start = ((), (), s32[]{:S(2)}) async-start(), calls=%async_computation.13 | async-start | bytes 1310720 | tf_op jit(solution)/shard_map/all_gather | solution.py:71
  834.1 253.6 %all-gather.67.cloned.1.call-start = ((), (), s32[]{:S(2)}) async-start(), calls=%async_computation.17 | async-start | bytes 1114112 | tf_op jit(solution)/shard_map/all_gather | solution.py:67
  854.6 6.6 copy-start.50
  864.2 233.3 %all-gather.75.cloned.1.call-start = ((), (), s32[]{:S(2)}) async-start(), calls=%async_computation.21 | async-start | bytes 1114112 | tf_op jit(solution)/shard_map/all_gather | solution.py:68
  903.4 216.8 %all-gather.49.cloned.1.call-start = ((), (), s32[]{:S(2)}) async-start(), calls=%async_computation.7 | async-start | bytes 1310720 | tf_op jit(solution)/shard_map/all_gather | solution.py:36
  1082.0 17.2 %copy-start.7 = (f32[128,512]{1,0:T(8,128)}, f32[128,512]{1,0:T(8,128)S(1)}, u32[]{:S(2)}) copy-start(f32[128,512]{1,0:T(8,128)S(1)} %fusion.135) | copy-start | bytes 786436
  1084.7 14.5 %copy-start.19 = (f32[128,512]{1,0:T(8,128)}, f32[128,512]{1,0:T(8,128)S(1)}, u32[]{:S(2)}) copy-start(f32[128,512]{1,0:T(8,128)S(1)} %fusion.133) | copy-start | bytes 786436
  1087.6 11.6 copy-start.31
  1092.2 5.3 copy-start.36
  1093.1 109.6 %all-gather.47.cloned.1.call-start = ((), (), s32[]{:S(2)}) async-start(), calls=%async_computation.5 | async-start | bytes 1310720 | tf_op jit(solution)/shard_map/all_gather | solution.py:36
  1102.0 19.9 %copy-start.37 = (f32[4,32,512]{2,1,0:T(8,128)S(1)}, f32[4,32,512]{2,1,0:T(8,128)}, u32[]{:S(2)}) copy-start(f32[4,32,512]{2,1,0:T(8,128)} %copy-done.36) | copy-start | bytes 786436
  1102.1 19.8 %copy-start.34 = (f32[4,32,512]{2,1,0:T(8,128)}, f32[4,32,512]{2,1,0:T(8,128)S(1)}, u32[]{:S(2)}) copy-start(f32[4,32,512]{2,1,0:T(8,128)S(1)} %pad_maximum_fusion.6) | copy-start | bytes 786436
  1103.0 118.3 %reduce-scatter.5.cloned.1.call-start = ((), (), s32[]{:S(2)}) async-start(), calls=%async_computation.8 | async-start | bytes 4456448 | tf_op jit(solution)/shard_map/reduce_scatter | solution.py:40
  1126.9 18.8 %copy-start.1 = (f32[128,512]{1,0:T(8,128)S(1)}, f32[128,512]{1,0:T(8,128)}, u32[]{:S(2)}) copy-start(f32[128,512]{1,0:T(8,128)} %copy-done) | copy-start | bytes 786436
  1126.9 18.8 %copy-start.13 = (f32[128,512]{1,0:T(8,128)S(1)}, f32[128,512]{1,0:T(8,128)}, u32[]{:S(2)}) copy-start(f32[128,512]{1,0:T(8,128)} %copy-done.11) | copy-start | bytes 786436
  1126.9 20.8 %copy-start.10 = (f32[512,3,32]{0,2,1:T(8,128)S(1)}, f32[512,3,32]{0,2,1:T(8,128)}, u32[]{:S(2)}) copy-start(f32[512,3,32]{0,2,1:T(8,128)} %copy-done.9) | copy-start | bytes 589828
  1126.9 37.9 %copy-start.4 = (f32[128,512]{1,0:T(8,128)S(1)}, f32[128,512]{1,0:T(8,128)}, u32[]{:S(2)}) copy-start(f32[128,512]{1,0:T(8,128)} %copy-done.2) | copy-start | bytes 786436
  1126.9 37.9 %copy-start.16 = (f32[128,512]{1,0:T(8,128)S(1)}, f32[128,512]{1,0:T(8,128)}, u32[]{:S(2)}) copy-start(f32[128,512]{1,0:T(8,128)} %copy-done.14) | copy-start | bytes 786436
  1126.9 55.7 %copy-start.6 = (f32[128,512]{1,0:T(8,128)S(1)}, f32[128,512]{1,0:T(8,128)}, u32[]{:S(2)}) copy-start(f32[128,512]{1,0:T(8,128)} %copy-done.5) | copy-start | bytes 786436
  1127.0 55.7 %copy-start.18 = (f32[128,512]{1,0:T(8,128)S(1)}, f32[128,512]{1,0:T(8,128)}, u32[]{:S(2)}) copy-start(f32[128,512]{1,0:T(8,128)} %copy-done.17) | copy-start | bytes 786436
  1127.0 169.8 %all-gather.77.cloned.1.call-start = ((), (), s32[]{:S(2)}) async-start(), calls=%async_computation.22 | async-start | bytes 2129920 | tf_op jit(solution)/shard_map/all_gather | solution.py:8
  1147.6 35.1 %copy-start.30 = (f32[128,512]{1,0:T(8,128)S(1)}, f32[128,512]{1,0:T(8,128)}, u32[]{:S(2)}) copy-start(f32[128,512]{1,0:T(8,128)} %copy-done.28) | copy-start | bytes 786436
  1147.6 53.2 %copy-start.8 = (f32[128,512]{1,0:T(8,128)S(1)}, f32[128,512]{1,0:T(8,128)}, u32[]{:S(2)}) copy-start(f32[128,512]{1,0:T(8,128)} %copy-done.7) | copy-start | bytes 786436
  1147.6 53.2 %copy-start.20 = (f32[128,512]{1,0:T(8,128)S(1)}, f32[128,512]{1,0:T(8,128)}, u32[]{:S(2)}) copy-start(f32[128,512]{1,0:T(8,128)} %copy-done.19) | copy-start | bytes 786436
  1147.6 53.2 %copy-start.32 = (f32[128,512]{1,0:T(8,128)S(1)}, f32[128,512]{1,0:T(8,128)}, u32[]{:S(2)}) copy-start(f32[128,512]{1,0:T(8,128)} %copy-done.31) | copy-start | bytes 786436
  1200.7 3.7 copy-start.35
  1202.7 157.5 %reduce-scatter.3.cloned.1.call-start = ((), (), s32[]{:S(2)}) async-start(), calls=%async_computation.6 | async-start | bytes 4456448 | tf_op jit(solution)/shard_map/reduce_scatter | solution.py:40
  1209.4 8.3 copy-start.33
  1209.4 8.3 copy-start.41
  1217.7 80.8 %copy-start.66 = (f32[64,64]{1,0:T(8,128)S(1)}, f32[64,64]{1,0:T(8,128)}, u32[]{:S(2)}) copy-start(f32[64,64]{1,0:T(8,128)} %param.38) | copy-start | bytes 49156
  1217.7 142.5 %copy-start.56 = (f32[1,4,1,32,4,1,128]{6,5,4,3,2,1,0:T(1,128)S(1)}, f32[1,4,1,32,4,1,128]{6,5,4,3,2,1,0:T(1,128)}, u32[]{:S(2)}) copy-start(f32[1,4,1,32,4,1,128]{6,5,4,3,2,1,0:T(1,128)} %param.36) | copy-start | bytes 786436
  1221.3 138.9 %collective-permute-start = (f32[128,512]{1,0:T(8,128)}, f32[128,512]{1,0:T(8,128)S(1)}, u32[]{:S(2)}, u32[]{:S(2)}) collective-permute-start(f32[128,512]{1,0:T(8,128)} %reduce-scatter.5.cloned.1.call-done), channel_id=1, source_target_pairs={{64,0},{128,64},{192,128},{65,1},{129,65},{193,129},{66,2},{130,66... | collective-permute-start | bytes 786440 | tf_op jit(solution)/shard_map/ppermute | solution.py:16
  (27 other events, 35.3 us)
Sparse Core Ops, SparseCore 0:
  10.4 41.4 all-gather.50
  54.3 24.2 all-gather.40
  226.5 46.1 all-gather.52
  298.3 24.3 all-gather.42
  479.5 37.4 all-gather.54
  519.2 39.8 all-gather.60
  560.9 37.2 all-gather.68
  600.6 24.2 all-gather.44
  626.7 40.1 all-gather.62
  668.6 37.2 all-gather.70
  783.5 27.0 all-gather.56
  812.3 39.7 all-gather.64
  853.9 37.1 all-gather.72
  892.8 24.2 all-gather.58
  918.9 40.2 all-gather.66
  960.9 37.0 all-gather.74
  1093.2 26.9 all-gather.48
  1121.9 27.0 all-gather.46
  1151.5 65.2 reduce-scatter.4
  1220.0 76.6 all-gather.76
  1299.3 60.8 reduce-scatter.2
